TPU v7x, 32 devices: a whole 2x2x4 slice. The times are simulated.
32 devices in a mesh: dp: 8 (over z, x), mp: 4 (over y, core).
Axes of the slice: x: 2, y: 2, z: 4, core: 2. Of those that a mesh axis runs over, the one named last changes fastest.
Arguments:
- tokens: bfloat16 [64, 256, 768], P(('dp', 'mp')), may hold values from -6 to 6
- cotangent: bfloat16 [64, 256, 768], P(('dp', 'mp')), may hold values from -6 to 6
- segment_ids: int32 [64, 256], P('dp'), may hold values from 0 to 32, as said below
- live_mask: int32 [64, 256], P('dp'), may hold values from 0 to 1, as said below
- expert_ids: int32 [64], P('dp'), may hold values from 0 to 1, as said below
- qkv_weight: bfloat16 [768, 3, 768], P(None, None, 'mp'), may hold values from -0.21875 to 0.21875
- out_weight: bfloat16 [768, 768], P('mp'), may hold values from -0.875 to 0.875
- in_weight: bfloat16 [2, 768, 3072], P(None, None, 'mp'), may hold values from -0.21875 to 0.21875
- down_weight: bfloat16 [2, 3072, 768], P(None, 'mp'), may hold values from -0.15625 to 0.15625
- gain_attn: float32 [768], replicated, may hold values from 0.5 to 1.5
- shift_attn: float32 [768], replicated, may hold values from -3 to 3
- gain_ffn: float32 [768], replicated, may hold values from 0.5 to 1.5
- shift_ffn: float32 [768], replicated, may hold values from -3 to 3
Outputs:
- output: bfloat16 [64, 256, 768], P(('dp', 'mp'))
- grad_tokens: float32 [64, 256, 768], P(('dp', 'mp'))
- counts: int32 [2], replicated
- grad_qkv_weight: float32 [768, 3, 768], P(None, None, 'mp')
- grad_out_weight: float32 [768, 768], P('mp')
- grad_in_weight: float32 [2, 768, 3072], P(None, None, 'mp')
- grad_down_weight: float32 [2, 3072, 768], P(None, 'mp')
- grad_gain_attn: float32 [768], replicated
- grad_shift_attn: float32 [768], replicated
- grad_gain_ffn: float32 [768], replicated
- grad_shift_ffn: float32 [768], replicated
Inputs may be any that keep to these rules, and one draw needn't show every extreme that they name: `segment_ids`: ids never fall along a row; the live slots with one id form one caption of 8 to 40 tokens, and captions of both lengths occur; padding slots carry the id 32. `live_mask`: each row is 1 on its first live slots and 0 on the padding after them; every row has live slots. `expert_ids`: every expert is named by some row.
All inputs are finite; a program needn't handle non-finite values.
Results may differ from a plain program's by a relative error of at most 0.018.
Values may be sent and summed in bfloat16 or wider, within the bound.
No kernel may reach another device: no remote copies, remote signals or barrier semaphores. Data moves between devices by JAX's collectives and lax.ppermute only.
A program may use at most 128 MiB of HBM per device.

v0:
```python
import jax
import jax.numpy as jnp
from jax import lax
from jax.sharding import PartitionSpec as P

HD = 64
norm_epsilon = 1e-05
masked_fill = -1e30


def layer_norm(values, norm_gain, norm_shift):
    average = jnp.mean(values, axis=-1, keepdims=True)
    centred = values - average
    variance = jnp.mean(centred * centred, axis=-1, keepdims=True)
    return centred * lax.rsqrt(variance + norm_epsilon) * norm_gain + norm_shift


def gelu_exact(values):
    return jax.nn.gelu(values, approximate=False)


def select_rows(values, hot_column):
    return values * hot_column[:, None, None]


def per_device(
    tokens,
    cotangent,
    segment_ids,
    live_mask,
    expert_ids,
    qkv_weight,
    out_weight,
    in_weight,
    down_weight,
    gain_attn,
    shift_attn,
    gain_ffn,
    shift_ffn,
):
    local_rows, slots, model_width = tokens.shape
    experts = in_weight.shape[0]
    heads_local = qkv_weight.shape[2] // HD
    score_scale = HD ** (-0.5)
    first_row = lax.axis_index("mp") * local_rows
    expert_hot = expert_ids[:, None] == jnp.arange(experts)[None, :]
    row_live = jnp.sum(live_mask, axis=1)
    local_counts = jnp.sum(jnp.where(expert_hot, row_live[:, None], 0), axis=0)
    counts = lax.psum(local_counts, "dp")
    hot_matrix = expert_hot.astype(jnp.bfloat16)
    token_float = tokens.astype(jnp.float32)
    norm_one = layer_norm(token_float, gain_attn, shift_attn).astype(jnp.bfloat16)
    norm_one_full = lax.all_gather(norm_one, "mp", axis=0, tiled=True)
    qkv_flat = qkv_weight.reshape(model_width, -1)
    qkv_all = jnp.einsum(
        "rsd,dk->rsk", norm_one_full, qkv_flat, preferred_element_type=jnp.float32
    ).astype(jnp.bfloat16)
    group_rows = qkv_all.shape[0]
    qkv_split = qkv_all.reshape(group_rows, slots, 3, heads_local, HD)
    queries = qkv_split[:, :, 0]
    key_part = qkv_split[:, :, 1]
    value_part = qkv_split[:, :, 2]
    same_caption = segment_ids[:, :, None] == segment_ids[:, None, :]
    diagonal = jnp.arange(slots)[:, None] == jnp.arange(slots)[None, :]
    allowed = (same_caption & ((live_mask[:, None, :] == 1) | diagonal[None]))[:, None]

    def masked_scores():
        raw_scores = (
            jnp.einsum("rqhd,rkhd->rhqk", queries, key_part, preferred_element_type=jnp.float32)
            * score_scale
        )
        return jnp.where(allowed, raw_scores, masked_fill)

    scores = masked_scores()
    row_top = jnp.max(scores, axis=-1, keepdims=True)
    exp_scores = jnp.exp(scores - row_top)
    row_total = jnp.sum(exp_scores, axis=-1, keepdims=True)
    attn_probs = exp_scores / row_total
    log_total = row_top + jnp.log(row_total)
    head_mix = jnp.einsum(
        "rhqk,rkhd->rqhd",
        attn_probs.astype(jnp.bfloat16),
        value_part,
        preferred_element_type=jnp.float32,
    )
    head_mix = head_mix.reshape(group_rows, slots, heads_local * HD).astype(jnp.bfloat16)
    picked = head_mix
    attn_local = lax.psum_scatter(
        jnp.einsum("rsk,kd->rsd", picked, out_weight, preferred_element_type=jnp.float32).astype(
            jnp.bfloat16
        ),
        "mp",
        scatter_dimension=0,
        tiled=True,
    ).astype(jnp.float32)
    residual = token_float + attn_local
    norm_two = layer_norm(residual, gain_ffn, shift_ffn).astype(jnp.bfloat16)
    norm_two_full = lax.all_gather(norm_two, "mp", axis=0, tiled=True)
    upward = jnp.zeros((group_rows, slots, in_weight.shape[2]), jnp.float32)
    for expert in range(experts):
        upward = upward + jnp.einsum(
            "rsd,df->rsf",
            select_rows(norm_two_full, hot_matrix[:, expert]),
            in_weight[expert],
            preferred_element_type=jnp.float32,
        )
    activated = gelu_exact(upward).astype(jnp.bfloat16)
    picked = activated
    hot_picked = hot_matrix
    total = jnp.zeros((local_rows * lax.axis_size("mp"), slots, model_width), jnp.float32)
    for ffn_expert in range(experts):
        total = total + jnp.einsum(
            "rsf,fd->rsd",
            select_rows(picked, hot_picked[:, ffn_expert]),
            down_weight[ffn_expert],
            preferred_element_type=jnp.float32,
        )
    ffn_local = lax.psum_scatter(
        total.astype(jnp.bfloat16), "mp", scatter_dimension=0, tiled=True
    ).astype(jnp.float32)
    output = (residual + ffn_local).astype(jnp.bfloat16)
    count_float = counts.astype(jnp.float32)
    loss_weight = jnp.sum(count_float) / (experts * count_float)
    local_hot = lax.dynamic_slice_in_dim(expert_hot, first_row, local_rows, 0)
    row_weight = jnp.sum(jnp.where(local_hot, loss_weight[None, :], 0.0), axis=1)
    live_local = lax.dynamic_slice_in_dim(live_mask, first_row, local_rows, 0)
    grad_output = (
        cotangent.astype(jnp.float32)
        * live_local[:, :, None].astype(jnp.float32)
        * row_weight[:, None, None]
    )
    grad_ffn_full = lax.all_gather(grad_output.astype(jnp.bfloat16), "mp", axis=0, tiled=True)
    grad_act = jnp.zeros(upward.shape, jnp.float32)
    down_list = []
    for expert in range(experts):
        masked_grad = select_rows(grad_ffn_full, hot_matrix[:, expert])
        grad_act = grad_act + jnp.einsum(
            "rsd,fd->rsf", masked_grad, down_weight[expert], preferred_element_type=jnp.float32
        )
        down_list.append(
            jnp.einsum("rsf,rsd->fd", activated, masked_grad, preferred_element_type=jnp.float32)
        )
    grad_down_weight = jnp.stack(down_list, axis=0)
    grad_up = jax.vjp(gelu_exact, upward)[1](grad_act)[0].astype(jnp.bfloat16)
    in_list = []
    for expert in range(experts):
        in_list.append(
            jnp.einsum(
                "rsd,rsf->df",
                select_rows(norm_two_full, hot_matrix[:, expert]),
                grad_up,
                preferred_element_type=jnp.float32,
            )
        )
    grad_in_weight = jnp.stack(in_list, axis=0)
    picked = grad_up
    hot_picked = hot_matrix
    total = jnp.zeros((local_rows * lax.axis_size("mp"), slots, model_width), jnp.float32)
    for expert in range(experts):
        total = total + jnp.einsum(
            "rsf,df->rsd",
            select_rows(picked, hot_picked[:, expert]),
            in_weight[expert],
            preferred_element_type=jnp.float32,
        )
    grad_norm_two = lax.psum_scatter(
        total.astype(jnp.bfloat16), "mp", scatter_dimension=0, tiled=True
    ).astype(jnp.float32)
    second_back = jax.vjp(layer_norm, residual, gain_ffn, shift_ffn)[1]
    grad_from_second, grad_gain_ffn, grad_shift_ffn = second_back(grad_norm_two)
    grad_residual = grad_output + grad_from_second
    grad_attn_full = lax.all_gather(grad_residual.astype(jnp.bfloat16), "mp", axis=0, tiled=True)
    grad_out_weight = jnp.einsum(
        "rsk,rsd->kd", head_mix, grad_attn_full, preferred_element_type=jnp.float32
    )
    grad_mix = jnp.einsum(
        "rsd,kd->rsk", grad_attn_full, out_weight, preferred_element_type=jnp.float32
    )
    grad_mix = grad_mix.astype(jnp.bfloat16).reshape(group_rows, slots, heads_local, HD)
    attn_again = jnp.exp(masked_scores() - log_total)
    grad_probs = jnp.einsum(
        "rqhd,rkhd->rhqk", grad_mix, value_part, preferred_element_type=jnp.float32
    )
    grad_scores = attn_again * (
        grad_probs - jnp.sum(grad_probs * attn_again, axis=-1, keepdims=True)
    )
    grad_scores = grad_scores.astype(jnp.bfloat16)
    grad_value = jnp.einsum(
        "rhqk,rqhd->rkhd",
        attn_again.astype(jnp.bfloat16),
        grad_mix,
        preferred_element_type=jnp.float32,
    )
    grad_query = (
        jnp.einsum("rhqk,rkhd->rqhd", grad_scores, key_part, preferred_element_type=jnp.float32)
        * score_scale
    )
    grad_key = (
        jnp.einsum("rhqk,rqhd->rkhd", grad_scores, queries, preferred_element_type=jnp.float32)
        * score_scale
    )
    grad_qkv = (
        jnp.stack([grad_query, grad_key, grad_value], axis=2)
        .astype(jnp.bfloat16)
        .reshape(group_rows, slots, -1)
    )
    grad_qkv_weight = jnp.einsum(
        "rsd,rsk->dk", norm_one_full, grad_qkv, preferred_element_type=jnp.float32
    )
    grad_qkv_weight = grad_qkv_weight.reshape(qkv_weight.shape)
    picked = grad_qkv
    grad_norm_one = lax.psum_scatter(
        jnp.einsum("rsk,dk->rsd", picked, qkv_flat, preferred_element_type=jnp.float32).astype(
            jnp.bfloat16
        ),
        "mp",
        scatter_dimension=0,
        tiled=True,
    ).astype(jnp.float32)
    first_back = jax.vjp(layer_norm, token_float, gain_attn, shift_attn)[1]
    grad_from_first, grad_gain_attn, grad_shift_attn = first_back(grad_norm_one)
    grad_tokens = grad_residual + grad_from_first
    norm_grads = lax.psum(
        (grad_gain_attn, grad_shift_attn, grad_gain_ffn, grad_shift_ffn), ("dp", "mp")
    )
    summed = lax.psum((grad_qkv_weight, grad_out_weight, grad_in_weight, grad_down_weight), "dp")
    return (
        output,
        grad_tokens,
        counts,
        summed[0],
        summed[1],
        summed[2],
        summed[3],
        norm_grads[0],
        norm_grads[1],
        norm_grads[2],
        norm_grads[3],
    )


def solution(mesh):
    in_specs = (
        P(("dp", "mp"), None, None),
        P(("dp", "mp"), None, None),
        P("dp", None),
        P("dp", None),
        P("dp"),
        P(None, None, "mp"),
        P("mp", None),
        P(None, None, "mp"),
        P(None, "mp", None),
        P(),
        P(),
        P(),
        P(),
    )
    out_specs = (
        P(("dp", "mp"), None, None),
        P(("dp", "mp"), None, None),
        P(),
        P(None, None, "mp"),
        P("mp", None),
        P(None, None, "mp"),
        P(None, "mp", None),
        P(),
        P(),
        P(),
        P(),
    )
    return jax.shard_map(
        per_device, mesh=mesh, in_specs=in_specs, out_specs=out_specs, check_vma=False
    )
```

profile of v0, /device:TPU:0, one launch (start us, length us, event | category | flops | bytes accessed | tf_op | source)
XLA Modules:
  0.0 761.4 jit_solution(12436911673130633448)
XLA Ops:
  7.3 1.4 convert_reduce_fusion.2
  8.6 1.5 fusion.70
  10.2 2.4 fusion.68
  12.7 0.7 or_and_fusion
  13.4 30.5 %all-gather.5.cloned.1.call-done = bf16[8,256,768]{2,1,0:T(8,128)(2,1)} async-done(((bf16[2,256,768]{2,1,0:T(8,128)(2,1)}), bf16[8,256,768]{2,1,0:T(8,128)(2,1)}) %all-gather.5.cloned.1.call-update) | async-done | bytes 3145744 | tf_op jit(solution)/shard_map/all_gather | solution.py:53
  44.0 3.9 convolution_convert_fusion.2
  47.9 1.3 fusion.125
  49.3 1.1 fusion.6
  50.4 1.5 copy-done.2
  51.9 1.2 fusion.95
  53.1 0.9 copy-done.10
  54.0 2.7 convolution_convert_fusion.1
  57.1 11.4 %psum.63 = s32[2]{0:T(128)S(1)} all-reduce(s32[2]{0:T(128)S(1)} %select_reduce_fusion), channel_id=1, replica_groups=mesh['dp'=8,'mp'=4] {'dp'}, use_global_device_ids=true, to_apply=%region_10.11 | all-reduce | flops 2 | bytes 16 | tf_op jit(solution)/shard_map/psum | solution.py:49
  68.4 0.6 convert_reduce_fusion.3
  69.0 0.7 multiply_divide_fusion
  69.8 1.1 fusion.74
  71.0 23.8 %reduce-scatter.5.cloned.1.call-done = bf16[2,256,768]{2,1,0:T(8,128)(2,1)} async-done(((bf16[8,256,768]{2,1,0:T(8,128)(2,1)}), bf16[2,256,768]{2,1,0:T(8,128)(2,1)}) %reduce-scatter.5.cloned.1.call-update) | async-done | bytes 786448 | tf_op jit(solution)/shard_map/reduce_scatter | solution.py:88
  94.8 1.5 fusion.97
  96.3 1.5 multiply_reduce_fusion.1
  97.9 1.3 add_convert_fusion.4
  99.5 26.0 %all-gather.9.cloned.1.call-done = bf16[8,256,768]{2,1,0:T(8,128)(2,1)} async-done(((bf16[2,256,768]{2,1,0:T(8,128)(2,1)}), bf16[8,256,768]{2,1,0:T(8,128)(2,1)}) %all-gather.9.cloned.1.call-update) | async-done | bytes 3145744 | tf_op jit(solution)/shard_map/all_gather | solution.py:132
  125.5 7.5 fusion.24
  133.0 23.0 %all-gather.7.cloned.1.call-done = bf16[8,256,768]{2,1,0:T(8,128)(2,1)} async-done(((bf16[2,256,768]{2,1,0:T(8,128)(2,1)}), bf16[8,256,768]{2,1,0:T(8,128)(2,1)}) %all-gather.7.cloned.1.call-update) | async-done | bytes 3145744 | tf_op jit(solution)/shard_map/all_gather | solution.py:98
  156.0 5.1 fusion.32
  161.1 4.6 fusion.88
  165.7 15.1 %multiply_convert_fusion.1 = (bf16[8,256,768]{2,1,0:T(8,128)(2,1)}, f32[8,256,768]{2,1,0:T(8,128)S(1)}) fusion(f32[8,256,768]{2,1,0:T(8,128)S(1)} %get-tuple-element.39, u8[256,768]{1,0:T(8,128)(4,1)S(1)} %get-tuple-element.12, u8[256,768]{1,0:T(8,128)(4,1)S(1)} %get-tuple-element.11), kind=kLoop, calls=%fused_computation.13 | loop fusion | flops 110100480 | bytes 16121856 | tf_op jit(solution)/shard_map/convert_element_type | solution.py:107
  180.8 10.6 %add_convert_fusion.1 = bf16[8,256,768]{2,1,0:T(8,128)(2,1)} fusion(f32[8,256,768]{2,1,0:T(8,128)S(1)} %get-tuple-element.30, f32[8,256,768]{2,1,0:T(8,128)} %fusion.24, f32[8,256,768]{2,1,0:T(8,128)S(1)} %get-tuple-element.39, bf16[8,256,768]{2,1,0:T(8,128)(2,1)} %all-gather.9.cloned.1.call-done, bf16[8]{0:T(256)(128)(2,1)S(1)} %get-tuple-element.35, ...), kind=kOutput, calls=%fused_computation.11 | convolution fusion | flops 2441084928 | bytes 26345488 | tf_op jit(solution)/shard_map/rsd,fd->rsf/dot_general | solution.py:137
  191.4 4.7 fusion.13
  196.2 4.1 add_convert_fusion
  200.3 38.0 %reduce-scatter.9.cloned.1.call-done = bf16[2,256,768]{2,1,0:T(8,128)(2,1)} async-done(((bf16[8,256,768]{2,1,0:T(8,128)(2,1)}), bf16[2,256,768]{2,1,0:T(8,128)(2,1)}) %reduce-scatter.9.cloned.1.call-update) | async-done | bytes 786448 | tf_op jit(solution)/shard_map/reduce_scatter | solution.py:166
  238.3 1.9 convert_reduce_fusion.1
  240.2 2.2 fusion.72
  242.4 2.8 fusion.115
  245.5 28.4 %all-gather.11.cloned.1.call-done = bf16[8,256,768]{2,1,0:T(8,128)(2,1)} async-done(((bf16[2,256,768]{2,1,0:T(8,128)(2,1)}), bf16[8,256,768]{2,1,0:T(8,128)(2,1)}) %all-gather.11.cloned.1.call-update) | async-done | bytes 3145744 | tf_op jit(solution)/shard_map/all_gather | solution.py:172
  273.9 3.2 convolution_convert_fusion.3
  277.2 4.0 fusion.92
  281.2 5.3 multiply_reduce_fusion
  286.5 4.6 multiply_convert_fusion
  291.1 1.1 multiply_bitcast_fusion
  292.2 0.7 multiply_bitcast_fusion.1
  292.9 0.3 maximum_convert_fusion
  293.1 1.4 copy-done.5
  294.6 0.3 copy.69
  294.9 4.1 convolution_convert_fusion
  299.0 5.1 fusion.17
  304.1 4.1 add_convert_fusion.2
  308.5 5.9 fusion.58
  314.5 2.8 fusion.55
  317.3 0.4 copy-done.22
  317.7 2.8 fusion.64
  320.5 2.8 fusion.61
  323.3 4.4 pad_maximum_fusion
  327.7 1.6 convolution_bitcast_fusion
  329.4 5.4 fusion.89
  334.8 2.2 reduce-scatter.11.cloned.1.call-done
  337.0 1.7 convert_reduce_fusion
  338.7 2.1 fusion.73
  340.8 39.9 %all-reduce = (f32[768]{0:T(1024)}, f32[768]{0:T(1024)}, f32[768]{0:T(1024)}, f32[768]{0:T(1024)}) all-reduce(f32[768]{0:T(1024)S(1)} %get-tuple-element.15, f32[768]{0:T(1024)S(1)} %get-tuple-element.19, f32[768]{0:T(1024)S(1)} %get-tuple-element.13, f32[768]{0:T(1024)S(1)} %get-tuple-element.17), channel_id=1, replica_groups=mesh['dp'=8,'mp'=4] {'dp','mp'}, use_global_device_ids=true, to_apply=%region_25.26 | all-reduce | flops 3072 | bytes 24576 | tf_op jit(solution)/shard_map/psum | solution.py:223
  380.7 3.7 add_add_fusion.2
  384.4 360.6 %all-reduce.4.cloned.1.call-done = (f32[768,3,192]{0,2,1:T(8,128)}, f32[192,768]{1,0:T(8,128)}, f32[2,768,768]{2,1,0:T(8,128)}, f32[2,768,768]{2,1,0:T(8,128)}) async-done(((f32[768,3,192]{0,2,1:T(8,128)}, f32[192,768]{1,0:T(8,128)}, f32[2,768,768]{2,1,0:T(8,128)}, f32[2,768,768]{2,1,0:T(8,128)}), (f32[768,3,192]{0,2,1:T(8,128)}, f32[192,768]{1,0:T(8,128)}, f32[2,768,768]{2,1,0:T(8,128)}, ...) | async-done | bytes 11796496 | tf_op jit(solution)/shard_map/psum | solution.py:226
  745.0 2.9 copy.95
  748.0 2.1 copy.96
  750.0 2.2 copy.97
  752.2 2.2 copy.98
  (104 shorter events, 1.8 us)
Async XLA Ops:
  7.2 36.8 %copy-start = (bf16[768,3,192]{0,2,1:T(8,128)(2,1)S(1)}, bf16[768,3,192]{0,2,1:T(8,128)(2,1)}, u32[]{:S(2)}) copy-start(bf16[768,3,192]{0,2,1:T(8,128)(2,1)} %param.18) | copy-start | bytes 2654212
  7.2 5.5 copy-start.19
  7.2 5.5 copy-start.20
  7.2 36.8 %all-gather.5.cloned.1.call-start = ((), (), s32[]{:S(2)}) async-start(), calls=%async_computation.4 | async-start | bytes 3932160 | tf_op jit(solution)/shard_map/all_gather | solution.py:53
  12.6 82.2 %reduce-scatter.5.cloned.1.call-start = ((), (), s32[]{:S(2)}) async-start(), calls=%async_computation.5 | async-start | bytes 3932160 | tf_op jit(solution)/shard_map/reduce_scatter | solution.py:88
  47.9 2.5 copy-start.14
  49.2 2.7 copy-start.2
  51.9 2.1 copy-start.16
  53.1 0.9 copy-start.10
  54.0 2.9 copy-start.27
  54.0 15.8 %copy-start.7 = (bf16[2,256,768]{2,1,0:T(8,128)(2,1)S(1)}, bf16[2,256,768]{2,1,0:T(8,128)(2,1)}, u32[]{:S(2)}) copy-start(bf16[2,256,768]{2,1,0:T(8,128)(2,1)} %param.14) | copy-start | bytes 2359300
  56.7 38.1 %copy-start.1 = (bf16[2,256,768]{2,1,0:T(8,128)(2,1)S(1)}, bf16[2,256,768]{2,1,0:T(8,128)(2,1)}, u32[]{:S(2)}) copy-start(bf16[2,256,768]{2,1,0:T(8,128)(2,1)} %param.13) | copy-start | bytes 2359300
  56.8 41.1 %copy-start.17 = (f32[768]{0:T(1024)S(1)}, f32[768]{0:T(1024)}, u32[]{:S(2)}) copy-start(f32[768]{0:T(1024)} %param.24) | copy-start | bytes 9220
  56.8 41.1 %copy-start.21 = (f32[768]{0:T(1024)S(1)}, f32[768]{0:T(1024)}, u32[]{:S(2)}) copy-start(f32[768]{0:T(1024)} %param.25) | copy-start | bytes 9220
  56.8 68.7 %all-gather.9.cloned.1.call-start = ((), (), s32[]{:S(2)}) async-start(), calls=%async_computation.8 | async-start | bytes 3932160 | tf_op jit(solution)/shard_map/all_gather | solution.py:132
  68.4 30.7 %copy-start.28 = (s32[2]{0:T(128)}, s32[2]{0:T(128)S(1)}, u32[]{:S(2)}) copy-start(s32[2]{0:T(128)S(1)} %psum.63) | copy-start | bytes 28
  71.0 85.0 %all-gather.7.cloned.1.call-start = ((), (), s32[]{:S(2)}) async-start(), calls=%async_computation.6 | async-start | bytes 3932160 | tf_op jit(solution)/shard_map/all_gather | solution.py:98
  94.8 3.1 copy-start.3
  99.2 139.1 %reduce-scatter.9.cloned.1.call-start = ((), (), s32[]{:S(2)}) async-start(), calls=%async_computation.9 | async-start | bytes 3932160 | tf_op jit(solution)/shard_map/reduce_scatter | solution.py:166
  156.0 5.1 copy-start.23
  156.0 5.1 copy-start.25
  191.4 4.7 copy-start.29
  200.3 73.6 %all-gather.11.cloned.1.call-start = ((), (), s32[]{:S(2)}) async-start(), calls=%async_computation.10 | async-start | bytes 3932160 | tf_op jit(solution)/shard_map/all_gather | solution.py:172
  238.3 4.1 copy-start.4
  245.3 91.8 %reduce-scatter.11.cloned.1.call-start = ((), (), s32[]{:S(2)}) async-start(), calls=%async_computation.11 | async-start | bytes 3932160 | tf_op jit(solution)/shard_map/reduce_scatter | solution.py:212
  273.9 7.3 slice-start
  277.2 4.1 slice-start.1
  286.5 4.6 copy-start.15
  293.1 1.5 copy-start.5
  299.0 81.7 %reduce-scatter.7.cloned.1.call-start = ((), (), s32[]{:S(2)}) async-start(), calls=%async_computation.7 | async-start | bytes 3932160 | tf_op jit(solution)/shard_map/reduce_scatter | solution.py:118
  299.0 5.1 copy-start.12
  299.0 5.1 copy-start.26
  308.2 436.8 %all-reduce.4.cloned.1.call-start = ((), (), s32[]{:S(2)}) async-start(), calls=%async_computation.12 | async-start | bytes 23592960 | tf_op jit(solution)/shard_map/psum | solution.py:226
  308.5 5.9 copy-start.24
  308.5 5.9 copy-start.30
  314.4 2.9 copy-start.13
  314.4 3.2 copy-start.22
  323.3 4.4 copy-start.9
  323.3 4.4 copy-start.11
  327.7 1.7 copy-start.6
  334.8 2.2 copy-start.18
  745.0 5.0 copy-start.8
  748.0 4.3 slice-start.2
  750.0 2.2 slice-start.3
Sparse Core Ops, SparseCore 0:
  12.7 31.2 all-gather.4
  56.9 37.8 reduce-scatter.4
  96.9 28.4 all-gather.8
  127.5 28.4 all-gather.6
  200.4 37.8 reduce-scatter.8
  245.4 28.5 all-gather.10
  299.1 37.8 reduce-scatter.10
  339.5 38.0 reduce-scatter.6
  382.8 362.1 all-reduce.3
where the time goes:
time: 769 us; the launch traced here: 761 us
  waiting for transfers between devices  533 us (69%)
  matrix products  94.5 us (12%)
  other arithmetic  52.9 us (7%)
  blocking collectives  51.2 us (7%)
  between operations  14.8 us (2%)
  local copies, waits for them, and re-layouts  14.1 us (2%)
    psum x1, waiting for transfers between devices, per_device(): lax.psum((grad_qkv_weight, grad_out_weight, grad_in_weight, grad_down_wei...  361 us
    psum x1, blocking collectives, per_device(): lax.psum((grad_gain_attn, grad_shift_attn, grad_gain_ffn, grad_shift_ffn)...  39.9 us
    reduce_scatter x2, waiting for transfers between devices, per_device(): lax.psum_scatter(total.astype(jnp.bfloat16), 'mp', scatter_dimension=0, t...  38 us
    all_gather x1, waiting for transfers between devices, per_device(): norm_one_full = lax.all_gather(norm_one, 'mp', axis=0, tiled=True)  30.5 us
    all_gather x1, waiting for transfers between devices, per_device(): lax.all_gather(grad_residual.astype(jnp.bfloat16), 'mp', axis=0, tiled=True)  28.4 us
    all_gather x1, waiting for transfers between devices, per_device(): lax.all_gather(grad_output.astype(jnp.bfloat16), 'mp', axis=0, tiled=True)  26 us
    reduce_scatter x1, waiting for transfers between devices, per_device(): lax.psum_scatter(jnp.einsum('rsk,kd->rsd', picked, out_weight, preferred_...  23.8 us
    all_gather x1, waiting for transfers between devices, per_device(): norm_two_full = lax.all_gather(norm_two, 'mp', axis=0, tiled=True)  23 us
  transfers between devices with their start and end apart: 9, of which 8 were waited for; matrix products, arithmetic and copies ran while one was open for 8% of the time, Pallas kernels for 0%

commit v1 on v0

--- a/solution.py
+++ b/solution.py
@@ -6,6 +6,12 @@
 HD = 64
 norm_epsilon = 1e-05
 masked_fill = -1e30
+
+
+def laid_out(pieces, dim):
+    pieces = jnp.moveaxis(pieces, 0, dim)
+    dims = pieces.shape
+    return pieces.reshape(*dims[:dim], dims[dim] * dims[dim + 1], *dims[dim + 2 :])
 
 
 def layer_norm(values, norm_gain, norm_shift):
@@ -129,7 +135,20 @@
         * live_local[:, :, None].astype(jnp.float32)
         * row_weight[:, None, None]
     )
-    grad_ffn_full = lax.all_gather(grad_output.astype(jnp.bfloat16), "mp", axis=0, tiled=True)
+    x = grad_output.astype(jnp.bfloat16)
+    size = lax.axis_size("mp")
+    pairs = [(i, (i + 1) % size) for i in range(size)]
+    back = [(b, a) for a, b in pairs]
+    lower, upper = ([], [])
+    for step in range(size - 1):
+        if step % 2 == 0:
+            lower.append(lax.ppermute(lower[-1] if lower else x, "mp", pairs))
+        else:
+            upper.append(lax.ppermute(upper[-1] if upper else x, "mp", back))
+    blocks = jnp.stack([*lower[::-1], x, *upper])
+    shift = lax.axis_index("mp") - len(lower)
+    blocks = blocks[(jnp.arange(size) - shift) % size]
+    grad_ffn_full = laid_out(blocks, 0)
     grad_act = jnp.zeros(upward.shape, jnp.float32)
     down_list = []
     for expert in range(experts):

time: 769 us -> 778 us (1.012)
  matrix products: 94.5 us -> 83.3 us
  other arithmetic: 52.9 us -> 62.5 us
    ppermute x0 -> x3, waiting for transfers between devices: none -> 39.2 us  [the longest x2 39.2 us: per_device(): lower.append(lax.ppermute(lower[-1] if lower else x, 'mp', pairs))]
    all_gather x1 -> x0, waiting for transfers between devices: 26 us -> none  [per_device(): lax.all_gather(grad_output.astype(jnp.bfloat16), 'mp', axis=0, tiled=True)]
    all_gather x1, waiting for transfers between devices: 23 us -> 0.01 us  [per_device(): norm_two_full = lax.all_gather(norm_two, 'mp', axis=0, tiled=True)]
    reduce_scatter x1, waiting for transfers between devices: 23.8 us -> 38 us  [per_device(): lax.psum_scatter(jnp.einsum('rsk,kd->rsd', picked, out_weight, preferred_...]
    unnamed x74 -> x80, local copies, waits for them, and re-layouts: 13.9 us -> 16.1 us
  transfers between devices with their start and end apart: 9 -> 11, of which waited for: 8 -> 8; matrix products, arithmetic and copies ran while one was open for 8% -> 8% of each run, Pallas kernels for 0% -> 0%
where the time goes in v1:
time: 778 us; the launch traced here: 771 us
  waiting for transfers between devices  535 us (69%)
  matrix products  83.3 us (11%)
  other arithmetic  62.5 us (8%)
  blocking collectives  51.7 us (7%)
  local copies, waits for them, and re-layouts  20.9 us (3%)
  between operations  15.1 us (2%)
    psum x1, waiting for transfers between devices, per_device(): lax.psum((grad_qkv_weight, grad_out_weight, grad_in_weight, grad_down_wei...  360 us
    psum x1, blocking collectives, per_device(): lax.psum((grad_gain_attn, grad_shift_attn, grad_gain_ffn, grad_shift_ffn)...  40.3 us
    ppermute x2, waiting for transfers between devices, per_device(): lower.append(lax.ppermute(lower[-1] if lower else x, 'mp', pairs))  39.2 us
    reduce_scatter x2, waiting for transfers between devices, per_device(): lax.psum_scatter(total.astype(jnp.bfloat16), 'mp', scatter_dimension=0, t...  38 us
    reduce_scatter x1, waiting for transfers between devices, per_device(): lax.psum_scatter(jnp.einsum('rsk,kd->rsd', picked, out_weight, preferred_...  38 us
    all_gather x1, waiting for transfers between devices, per_device(): norm_one_full = lax.all_gather(norm_one, 'mp', axis=0, tiled=True)  30.5 us
    all_gather x1, waiting for transfers between devices, per_device(): lax.all_gather(grad_residual.astype(jnp.bfloat16), 'mp', axis=0, tiled=True)  28.4 us
    unnamed x80, local copies, waits for them, and re-layouts  16.1 us
  transfers between devices with their start and end apart: 11, of which 8 were waited for; matrix products, arithmetic and copies ran while one was open for 8% of the time, Pallas kernels for 0%

profile of v1, /device:TPU:0, one launch (start us, length us, event | category | flops | bytes accessed | tf_op | source)
XLA Modules:
  0.0 770.9 jit_solution(15547384919574644097)
XLA Ops:
  7.3 1.4 convert_reduce_fusion.2
  8.6 1.5 fusion.54
  10.2 2.4 fusion.52
  12.7 0.7 or_and_fusion
  13.4 30.5 %all-gather.4.cloned.1.call-done = bf16[8,256,768]{2,1,0:T(8,128)(2,1)} async-done(((bf16[2,256,768]{2,1,0:T(8,128)(2,1)}), bf16[8,256,768]{2,1,0:T(8,128)(2,1)}) %all-gather.4.cloned.1.call-update) | async-done | bytes 3145744 | tf_op jit(solution)/shard_map/all_gather | solution.py:59
  44.0 3.9 convolution_convert_fusion.2
  47.9 1.3 fusion.108
  49.2 1.1 fusion.6
  50.4 1.5 copy-done.2
  51.9 1.2 fusion.75
  53.2 2.7 convolution_convert_fusion.1
  56.0 38.0 %reduce-scatter.5.cloned.1.call-done = bf16[2,256,768]{2,1,0:T(8,128)(2,1)} async-done(((bf16[8,256,768]{2,1,0:T(8,128)(2,1)}), bf16[2,256,768]{2,1,0:T(8,128)(2,1)}) %reduce-scatter.5.cloned.1.call-update) | async-done | bytes 786448 | tf_op jit(solution)/shard_map/reduce_scatter | solution.py:94
  93.9 1.5 fusion.77
  95.4 1.5 multiply_reduce_fusion.1
  97.0 1.3 add_convert_fusion.4
  98.6 11.4 %psum.63 = s32[2]{0:T(128)S(1)} all-reduce(s32[2]{0:T(128)S(1)} %select_reduce_fusion), channel_id=1, replica_groups=mesh['dp'=8,'mp'=4] {'dp'}, use_global_device_ids=true, to_apply=%region_10.11 | all-reduce | flops 2 | bytes 16 | tf_op jit(solution)/shard_map/psum | solution.py:55
  111.3 1.1 fusion.58
  112.5 1.7 collective-permute-start.2
  114.2 27.9 %collective-permute-done = bf16[2,256,768]{2,1,0:T(8,128)(2,1)} collective-permute-done((bf16[2,256,768]{2,1,0:T(8,128)(2,1)}, bf16[2,256,768]{2,1,0:T(8,128)(2,1)}, u32[]{:S(2)}, u32[]{:S(2)}) %collective-permute-start) | collective-permute-done | bytes 786464 | tf_op jit(solution)/shard_map/ppermute | solution.py:145
  142.8 11.2 %collective-permute-done.1 = bf16[2,256,768]{2,1,0:T(8,128)(2,1)} collective-permute-done((bf16[2,256,768]{2,1,0:T(8,128)(2,1)}, bf16[2,256,768]{2,1,0:T(8,128)(2,1)}, u32[]{:S(2)}, u32[]{:S(2)}) %collective-permute-start.1) | collective-permute-done | bytes 786464 | tf_op jit(solution)/shard_map/ppermute | solution.py:145
  154.1 3.1 pad_maximum_fusion.2
  157.2 4.3 gather_fusion
  161.5 4.2 broadcast_multiply_fusion
  165.6 4.5 fusion.80
  170.2 5.1 fusion.24
  175.3 4.5 fusion.68
  179.8 14.7 %multiply_convert_fusion.1 = (bf16[8,256,768]{2,1,0:T(8,128)(2,1)}, f32[8,256,768]{2,1,0:T(8,128)S(1)}) fusion(f32[8,256,768]{2,1,0:T(8,128)S(1)} %get-tuple-element.45, u8[256,768]{1,0:T(8,128)(4,1)S(1)} %get-tuple-element.12, u8[256,768]{1,0:T(8,128)(4,1)S(1)} %get-tuple-element.11), kind=kLoop, calls=%fused_computation.14 | loop fusion | flops 110100480 | bytes 16121856 | tf_op jit(solution)/shard_map/convert_element_type | solution.py:113
  194.5 8.3 %add_convert_fusion.1 = bf16[8,256,768]{2,1,0:T(8,128)(2,1)} fusion(f32[8,256,768]{2,1,0:T(8,128)S(1)} %get-tuple-element.32, f32[8,256,768]{2,1,0:T(8,128)} %fusion.80, f32[8,256,768]{2,1,0:T(8,128)S(1)} %get-tuple-element.45, bf16[8,256,768]{2,1,0:T(8,128)(2,1)S(1)} %bitcast.148, bf16[2,768,768]{2,1,0:T(8,128)(2,1)} %param.21), kind=kOutput, calls=%fused_computation.12 | convolution fusion | flops 2439512064 | bytes 26345472 | tf_op jit(solution)/shard_map/rsd,fd->rsf/dot_general | solution.py:156
  202.8 5.1 fusion.13
  207.9 4.1 add_convert_fusion
  212.1 38.0 %reduce-scatter.9.cloned.1.call-done = bf16[2,256,768]{2,1,0:T(8,128)(2,1)} async-done(((bf16[8,256,768]{2,1,0:T(8,128)(2,1)}), bf16[2,256,768]{2,1,0:T(8,128)(2,1)}) %reduce-scatter.9.cloned.1.call-update) | async-done | bytes 786448 | tf_op jit(solution)/shard_map/reduce_scatter | solution.py:185
  250.1 1.9 convert_reduce_fusion.1
  251.9 2.2 fusion.56
  254.1 1.7 fusion.96
  256.1 28.4 %all-gather.8.cloned.1.call-done = bf16[8,256,768]{2,1,0:T(8,128)(2,1)} async-done(((bf16[2,256,768]{2,1,0:T(8,128)(2,1)}), bf16[8,256,768]{2,1,0:T(8,128)(2,1)}) %all-gather.8.cloned.1.call-update) | async-done | bytes 3145744 | tf_op jit(solution)/shard_map/all_gather | solution.py:191
  284.5 3.2 convolution_convert_fusion.3
  287.8 7.0 multiply_reduce_fusion
  294.9 4.5 multiply_convert_fusion
  300.0 1.1 multiply_bitcast_fusion
  301.0 1.1 fusion.72
  302.4 1.4 copy-done.6
  304.2 4.1 convolution_convert_fusion
  308.3 5.1 fusion.17
  313.4 4.1 add_convert_fusion.2
  317.8 2.6 bitcast_multiply_fusion.1
  320.8 2.8 convolution_bitcast_fusion
  323.5 2.7 convolution_bitcast_fusion.1
  326.3 2.7 pad_maximum_fusion.1
  329.0 0.7 copy-done.25
  329.7 1.1 copy-done.33
  330.8 2.8 fusion.45
  333.7 2.8 fusion.48
  336.6 2.7 pad_maximum_fusion
  340.3 1.6 convolution_bitcast_fusion.2
  342.2 3.5 fusion.69
  346.4 1.7 convert_reduce_fusion
  348.1 2.1 fusion.57
  350.2 40.3 %all-reduce = (f32[768]{0:T(1024)}, f32[768]{0:T(1024)}, f32[768]{0:T(1024)}, f32[768]{0:T(1024)}) all-reduce(f32[768]{0:T(1024)S(1)} %get-tuple-element.15, f32[768]{0:T(1024)S(1)} %get-tuple-element.19, f32[768]{0:T(1024)S(1)} %get-tuple-element.13, f32[768]{0:T(1024)S(1)} %get-tuple-element.17), channel_id=1, replica_groups=mesh['dp'=8,'mp'=4] {'dp','mp'}, use_global_device_ids=true, to_apply=%region_25.26 | all-reduce | flops 3072 | bytes 24576 | tf_op jit(solution)/shard_map/psum | solution.py:242
  390.5 3.7 add_add_fusion.2
  394.2 360.0 %all-reduce.4.cloned.1.call-done = (f32[768,3,192]{0,2,1:T(8,128)}, f32[192,768]{1,0:T(8,128)}, f32[2,768,768]{2,1,0:T(8,128)}, f32[2,768,768]{2,1,0:T(8,128)}) async-done(((f32[768,3,192]{0,2,1:T(8,128)}, f32[192,768]{1,0:T(8,128)}, f32[2,768,768]{2,1,0:T(8,128)}, f32[2,768,768]{2,1,0:T(8,128)}), (f32[768,3,192]{0,2,1:T(8,128)}, f32[192,768]{1,0:T(8,128)}, f32[2,768,768]{2,1,0:T(8,128)}, ...) | async-done | bytes 11796496 | tf_op jit(solution)/shard_map/psum | solution.py:245
  754.3 2.9 copy.95
  757.2 2.1 copy.96
  759.3 2.2 copy.97
  761.5 2.2 copy.98
  (123 shorter events, 6.9 us)
Async XLA Ops:
  7.2 36.8 %copy-start = (bf16[768,3,192]{0,2,1:T(8,128)(2,1)S(1)}, bf16[768,3,192]{0,2,1:T(8,128)(2,1)}, u32[]{:S(2)}) copy-start(bf16[768,3,192]{0,2,1:T(8,128)(2,1)} %param.18) | copy-start | bytes 2654212
  7.2 5.5 copy-start.20
  7.2 5.5 copy-start.21
  7.2 36.8 %all-gather.4.cloned.1.call-start = ((), (), s32[]{:S(2)}) async-start(), calls=%async_computation.4 | async-start | bytes 3932160 | tf_op jit(solution)/shard_map/all_gather | solution.py:59
  12.6 81.4 %reduce-scatter.5.cloned.1.call-start = ((), (), s32[]{:S(2)}) async-start(), calls=%async_computation.5 | async-start | bytes 3932160 | tf_op jit(solution)/shard_map/reduce_scatter | solution.py:94
  47.9 2.5 copy-start.15
  49.2 2.7 copy-start.2
  51.9 1.2 copy-start.17
  53.1 2.8 copy-start.11
  53.2 40.8 %copy-start.1 = (bf16[2,256,768]{2,1,0:T(8,128)(2,1)S(1)}, bf16[2,256,768]{2,1,0:T(8,128)(2,1)}, u32[]{:S(2)}) copy-start(bf16[2,256,768]{2,1,0:T(8,128)(2,1)} %param.13) | copy-start | bytes 2359300
  55.9 41.1 %copy-start.18 = (f32[768]{0:T(1024)S(1)}, f32[768]{0:T(1024)}, u32[]{:S(2)}) copy-start(f32[768]{0:T(1024)} %param.24) | copy-start | bytes 9220
  55.9 41.1 %copy-start.22 = (f32[768]{0:T(1024)S(1)}, f32[768]{0:T(1024)}, u32[]{:S(2)}) copy-start(f32[768]{0:T(1024)} %param.25) | copy-start | bytes 9220
  55.9 42.6 %copy-start.30 = (s32[8]{0:T(128)S(1)}, s32[8]{0:T(128)}, u32[]{:S(2)}) copy-start(s32[8]{0:T(128)} %param.17) | copy-start | bytes 100
  55.9 55.4 %copy-start.4 = (bf16[2,256,768]{2,1,0:T(8,128)(2,1)S(1)}, bf16[2,256,768]{2,1,0:T(8,128)(2,1)}, u32[]{:S(2)}) copy-start(bf16[2,256,768]{2,1,0:T(8,128)(2,1)} %param.14) | copy-start | bytes 2359300
  55.9 114.3 %all-gather.6.cloned.1.call-start = ((), (), s32[]{:S(2)}) async-start(), calls=%async_computation.6 | async-start | bytes 3932160 | tf_op jit(solution)/shard_map/all_gather | solution.py:104
  93.9 3.1 copy-start.3
  98.3 151.7 %reduce-scatter.9.cloned.1.call-start = ((), (), s32[]{:S(2)}) async-start(), calls=%async_computation.8 | async-start | bytes 3932160 | tf_op jit(solution)/shard_map/reduce_scatter | solution.py:185
  110.0 47.2 %copy-start.31 = (s32[2]{0:T(128)}, s32[2]{0:T(128)S(1)}, u32[]{:S(2)}) copy-start(s32[2]{0:T(128)S(1)} %psum.63) | copy-start | bytes 28
  112.5 29.7 %collective-permute-start = (bf16[2,256,768]{2,1,0:T(8,128)(2,1)}, bf16[2,256,768]{2,1,0:T(8,128)(2,1)}, u32[]{:S(2)}, u32[]{:S(2)}) collective-permute-start(bf16[2,256,768]{2,1,0:T(8,128)(2,1)} %fusion.58), channel_id=1, source_target_pairs={{0,1},{1,2},{2,3},{3,0},{4,5},{5,6},{6,7},{7,4},{8,9},{9,10},{10,1... | collective-permute-start | bytes 2359304 | tf_op jit(solution)/shard_map/ppermute | solution.py:145
  112.5 30.4 %collective-permute-start.2 = (bf16[2,256,768]{2,1,0:T(8,128)(2,1)}, bf16[2,256,768]{2,1,0:T(8,128)(2,1)}, u32[]{:S(2)}, u32[]{:S(2)}) collective-permute-start(bf16[2,256,768]{2,1,0:T(8,128)(2,1)} %fusion.58), channel_id=1, source_target_pairs={{1,0},{2,1},{3,2},{0,3},{5,4},{6,5},{7,6},{4,7},{9,8},{10,9},{11,1... | collective-permute-start | bytes 2359304 | tf_op jit(solution)/shard_map/ppermute | solution.py:147
  142.1 11.9 %collective-permute-start.1 = (bf16[2,256,768]{2,1,0:T(8,128)(2,1)}, bf16[2,256,768]{2,1,0:T(8,128)(2,1)}, u32[]{:S(2)}, u32[]{:S(2)}) collective-permute-start(bf16[2,256,768]{2,1,0:T(8,128)(2,1)} %collective-permute-done), channel_id=1, source_target_pairs={{0,1},{1,2},{2,3},{3,0},{4,5},{5,6},{6,7},{7,4},{8,9},{9,10},{10,1... | collective-permute-start | bytes 2359304 | tf_op jit(solution)/shard_map/ppermute | solution.py:145
  161.5 4.2 copy-start.28
  170.2 5.1 copy-start.24
  170.2 5.1 copy-start.26
  179.8 14.7 %copy-start.9 = (bf16[4,2,256,768]{3,2,1,0:T(8,128)(2,1)S(1)}, bf16[4,2,256,768]{3,2,1,0:T(8,128)(2,1)}, u32[]{:S(2)}) copy-start(bf16[4,2,256,768]{3,2,1,0:T(8,128)(2,1)} %get-tuple-element.35) | copy-start | bytes 9437188
  202.8 5.1 copy-start.27
  202.8 5.1 copy-start.32
  212.0 72.5 %all-gather.8.cloned.1.call-start = ((), (), s32[]{:S(2)}) async-start(), calls=%async_computation.9 | async-start | bytes 3932160 | tf_op jit(solution)/shard_map/all_gather | solution.py:191
  250.1 4.1 copy-start.5
  255.9 90.4 %reduce-scatter.11.cloned.1.call-start = ((), (), s32[]{:S(2)}) async-start(), calls=%async_computation.10 | async-start | bytes 3932160 | tf_op jit(solution)/shard_map/reduce_scatter | solution.py:231
  284.5 3.2 copy-start.16
  287.8 7.1 slice-start
  287.8 7.1 slice-start.1
  302.4 1.4 copy-start.6
  308.2 82.3 %reduce-scatter.7.cloned.1.call-start = ((), (), s32[]{:S(2)}) async-start(), calls=%async_computation.7 | async-start | bytes 3932160 | tf_op jit(solution)/shard_map/reduce_scatter | solution.py:124
  308.3 5.1 copy-start.13
  308.3 5.1 copy-start.29
  317.5 436.7 %all-reduce.4.cloned.1.call-start = ((), (), s32[]{:S(2)}) async-start(), calls=%async_computation.11 | async-start | bytes 23592960 | tf_op jit(solution)/shard_map/psum | solution.py:245
  317.8 3.0 copy-start.14
  326.3 3.5 copy-start.25
  326.3 4.6 copy-start.33
  336.5 3.4 copy-start.10
  336.5 3.8 copy-start.12
  336.6 5.4 copy-start.23
  340.3 1.9 copy-start.7
  345.7 0.7 copy-start.19
  754.3 5.0 copy-start.8
  757.2 4.3 slice-start.2
  759.3 2.2 slice-start.3
Sparse Core Ops, SparseCore 0:
  12.7 31.2 all-gather.3
  56.0 37.8 reduce-scatter.4
  98.5 38.2 all-gather.5
  212.2 37.8 reduce-scatter.8
  256.0 28.4 all-gather.7
  308.4 37.8 reduce-scatter.10
  348.8 38.0 reduce-scatter.6
  392.1 362.1 all-reduce.3
